TPU v7x, 128 devices: a whole 4x4x4 slice. The times are simulated.
128 devices in a mesh: dp: 16 (over x, y), fsdp: 8 (over z, core).
Axes of the slice: x: 4, y: 4, z: 4, core: 2. Of those that a mesh axis runs over, the one named last changes fastest.
Arguments:
- page_embed: bfloat16 [81920, 2048], P(('dp', 'fsdp')), may hold values from -6 to 6
- page_slot: int32 [81920], P(('dp', 'fsdp')), may hold values from 0 to 10239, as said below
- doc_ids: int32 [128, 640], P(('dp', 'fsdp')), may hold values from 0 to 9, never falling along the last dimension, each value on 1 to 128 neighbouring positions
- qkv_weight: bfloat16 [3, 2048, 1024], P(None, 'fsdp'), may hold values from -0.125 to 0.125
- out_weight: bfloat16 [1024, 2048], P(None, 'fsdp'), may hold values from -0.1875 to 0.1875
- fig_slot: int32 [2048], P(('dp', 'fsdp')), may hold values from 0 to 639
- cap_slot: int32 [2048], P(('dp', 'fsdp')), may hold values from 0 to 639
- logit_scale: float32 [1], replicated, may hold values from 10 to 30
- loss_cotangent: float32 [2048], P(('dp', 'fsdp')), may hold values from 8 to 64
Outputs:
- page_grad: bfloat16 [81920, 2048], P(('dp', 'fsdp'))
- pair_loss: float32 [2048], P(('dp', 'fsdp'))
Inputs may be any that keep to these rules, and one draw needn't show every extreme that they name: page_slot // 640 is the dp index of the owner and page_slot % 640 the slot there; within each group every slot is named by exactly one page; one device sends at most 50 pages to one owner, and every device sends exactly 50 to some owners. `doc_ids`: along a device's slots the document number never falls; each of the 10 documents has 1 to 128 slots, one exactly 128. `fig_slot`: a slot of the pair's own device. `cap_slot`: a slot of the pair's own device.
All inputs are finite; a program needn't handle non-finite values.
Results may differ from a plain program's by a relative error of at most 0.017.
Values may be sent and summed in bfloat16 or wider, within the bound.
No kernel may reach another device: no remote copies, remote signals or barrier semaphores. Data moves between devices by JAX's collectives and lax.ppermute only.
A program may use at most 192 MiB of HBM per device.

v0:
```python
import math
import jax
import jax.numpy as jnp
from jax import lax
from jax.sharding import PartitionSpec as P

HD = 64
EPSILON = 1e-06


def log_total(values, axis):
    return jnp.log(jnp.sum(jnp.exp(values), axis=axis))


def attend(query_h, key_value, out_mat, query_doc, doc_row):
    query_count = query_h.shape[0]
    row_count = key_value.shape[0]
    head_width = query_h.shape[1]
    query_h = query_h.reshape(query_count, -1, HD)
    key_h = key_value[:, :head_width].reshape(row_count, -1, HD)
    value_h = key_value[:, head_width:].reshape(row_count, -1, HD)
    scores = jnp.einsum("qhd,khd->hqk", query_h, key_h, preferred_element_type=jnp.float32) * (
        1.0 / math.sqrt(HD)
    )
    same_doc = query_doc[:, None] == doc_row[None, :]
    scores = jnp.where(same_doc[None], scores, -1e30)
    weights = jnp.exp(scores)
    attn_prob = (weights / jnp.sum(weights, axis=2, keepdims=True)).astype(jnp.bfloat16)
    mixed = jnp.einsum("hqk,khd->qhd", attn_prob, value_h, preferred_element_type=jnp.float32)
    mixed = mixed.astype(jnp.bfloat16).reshape(query_count, -1)
    return jnp.dot(mixed, out_mat, preferred_element_type=jnp.float32)


def select_rows(onehot, rows):
    picked = jnp.dot(onehot, rows, preferred_element_type=jnp.float32)
    return picked.astype(rows.dtype)


def select_rows_t(onehot, rows):
    picked = lax.dot_general(
        onehot, rows, (((0,), (0,)), ((), ())), preferred_element_type=jnp.float32
    )
    return picked.astype(rows.dtype)


def body(
    page_embed,
    page_slot,
    doc_ids,
    qkv_weight,
    out_weight,
    fig_slot,
    cap_slot,
    logit_scale,
    loss_cotangent,
):
    dp_count = lax.axis_size("dp")
    row_count = page_embed.shape[0]
    feature_width = page_embed.shape[1]
    capacity = 5 * row_count // (4 * dp_count)
    buffer_rows = dp_count * capacity
    owner_idx = page_slot // row_count
    slot_idx = page_slot % row_count
    onehot = (owner_idx[:, None] == jnp.arange(dp_count)[None, :]).astype(jnp.int32)
    rank_idx = jnp.sum((jnp.cumsum(onehot, axis=0) - onehot) * onehot, axis=1)
    dest = owner_idx * capacity + rank_idx
    send_match = dest[None, :] == jnp.arange(buffer_rows)[:, None]
    send_ids = jnp.where(
        jnp.any(send_match, axis=1),
        jnp.sum(jnp.where(send_match, slot_idx[None, :], 0), axis=1),
        row_count,
    ).reshape(dp_count, capacity)
    send_onehot = jnp.concatenate(
        [
            send_match.astype(jnp.bfloat16).reshape(dp_count, capacity, row_count),
            jnp.zeros((dp_count, 1, row_count), jnp.bfloat16),
        ],
        axis=1,
    )
    id_lanes = jnp.zeros((dp_count, feature_width), jnp.float32)
    id_lanes = id_lanes.at[:, :capacity].set((send_ids // 16).astype(jnp.float32))
    id_lanes = id_lanes.at[:, 128 : 128 + capacity].set((send_ids % 16).astype(jnp.float32))
    id_rows = jnp.concatenate(
        [jnp.zeros((dp_count, capacity, feature_width), jnp.float32), id_lanes[:, None, :]], axis=1
    )
    send_rows = (
        jnp.einsum("opk,kd->opd", send_onehot, page_embed, preferred_element_type=jnp.float32)
        + id_rows
    ).astype(jnp.bfloat16)
    recv_rows = lax.all_to_all(send_rows, "dp", split_axis=0, concat_axis=0, tiled=True)
    id_row = recv_rows[:, capacity, :].astype(jnp.float32)
    recv_ids = id_row[:, :capacity].astype(jnp.int32) * 16 + id_row[:, 128 : 128 + capacity].astype(
        jnp.int32
    )
    recv_ids = jnp.concatenate([recv_ids, jnp.full((dp_count, 1), row_count, jnp.int32)], axis=1)
    recv_onehot = (jnp.arange(row_count)[:, None, None] == recv_ids[None, :, :]).astype(
        jnp.bfloat16
    )
    slot_row_block = jnp.einsum(
        "sop,opd->sd", recv_onehot, recv_rows, preferred_element_type=jnp.float32
    ).astype(jnp.bfloat16)
    qkv_full, out_full = (
        lax.all_gather(qkv_weight, "fsdp", axis=1, tiled=True),
        lax.all_gather(out_weight, "fsdp", axis=1, tiled=True),
    )
    kv_full = jnp.concatenate([qkv_full[1], qkv_full[2]], axis=1)
    doc_row = doc_ids[0]
    pair_count = fig_slot.shape[0]
    query_slots = jnp.concatenate([fig_slot, cap_slot], axis=0)
    query_onehot = (query_slots[:, None] == jnp.arange(row_count)[None, :]).astype(jnp.bfloat16)
    query_doc = jnp.sum(
        jnp.where(query_slots[:, None] == jnp.arange(row_count)[None, :], doc_row[None, :], 0),
        axis=1,
    )
    query_rows = select_rows(query_onehot, slot_row_block)
    query_h = jnp.dot(query_rows, qkv_full[0], preferred_element_type=jnp.float32).astype(
        jnp.bfloat16
    )
    key_value = jnp.dot(slot_row_block, kv_full, preferred_element_type=jnp.float32).astype(
        jnp.bfloat16
    )

    def branch(query_in, key_value_in):
        return attend(query_in, key_value_in, out_full, query_doc, doc_row)

    attn_out, pullback = jax.vjp(branch, query_h, key_value)
    query_output = query_rows.astype(jnp.float32) + attn_out
    fig_vec = query_output[:pair_count]
    cap_vec = query_output[pair_count:]
    fig_inv = lax.rsqrt(jnp.sum(fig_vec * fig_vec, axis=1, keepdims=True) + EPSILON)
    cap_inv = lax.rsqrt(jnp.sum(cap_vec * cap_vec, axis=1, keepdims=True) + EPSILON)
    fig_unit = fig_vec * fig_inv
    cap_unit = cap_vec * cap_inv
    fig_emb = fig_unit.astype(jnp.bfloat16)
    cap_emb = cap_unit.astype(jnp.bfloat16)
    weight_hi = loss_cotangent.astype(jnp.bfloat16)
    weight_lo = (loss_cotangent - weight_hi.astype(jnp.float32)).astype(jnp.bfloat16)
    weight_lanes = jnp.zeros((2 * pair_count, 128), jnp.bfloat16)
    weight_lanes = weight_lanes.at[:pair_count, 0].set(weight_hi).at[:pair_count, 1].set(weight_lo)
    both_emb = jnp.concatenate([jnp.concatenate([fig_emb, cap_emb], axis=0), weight_lanes], axis=1)
    all_both = lax.all_to_all(
        jnp.broadcast_to(both_emb[None], (dp_count,) + both_emb.shape),
        "dp",
        split_axis=0,
        concat_axis=0,
        tiled=True,
    )
    all_fig = all_both[:, :pair_count, :feature_width].reshape(-1, feature_width)
    all_cap = all_both[:, pair_count:, :feature_width].reshape(-1, feature_width)
    all_weight = (
        all_both[:, :pair_count, feature_width].astype(jnp.float32)
        + all_both[:, :pair_count, feature_width + 1].astype(jnp.float32)
    ).reshape(-1)
    logit_mult = logit_scale[0]
    pair_total = all_fig.shape[0]
    first_pair = lax.axis_index("dp") * pair_count
    logits = logit_mult * jnp.dot(all_fig, all_cap.T, preferred_element_type=jnp.float32)
    row_lse = log_total(logits, 1)
    col_lse = log_total(logits, 0)
    eye_mat = jnp.eye(pair_total, dtype=jnp.float32)
    diag_logit = jnp.sum(logits * eye_mat, axis=1)
    own_rows = first_pair + jnp.arange(pair_count)
    own_mask = (jnp.arange(pair_total)[None, :] == own_rows[:, None]).astype(jnp.float32)
    loss_all = 0.5 * (row_lse - diag_logit) + 0.5 * (col_lse - diag_logit)
    pair_loss = jnp.dot(own_mask, loss_all, precision=lax.Precision.HIGHEST)
    prob_rows = jnp.exp(logits - row_lse[:, None])
    prob_cols = jnp.exp(logits - col_lse[None, :])
    coef = (
        0.5 * all_weight[:, None] * (prob_rows - eye_mat)
        + 0.5 * (prob_cols - eye_mat) * all_weight[None, :]
    )
    coef_rows = jnp.dot(own_mask, coef, precision=lax.Precision.HIGHEST)
    coef_cols = jnp.dot(own_mask, coef.T, precision=lax.Precision.HIGHEST)
    fig_grad = logit_mult * jnp.dot(
        coef_rows, all_cap.astype(jnp.float32), precision=lax.Precision.HIGHEST
    )
    cap_grad = logit_mult * jnp.dot(
        coef_cols, all_fig.astype(jnp.float32), precision=lax.Precision.HIGHEST
    )
    figure_direction = fig_inv * (
        fig_grad - fig_unit * jnp.sum(fig_unit * fig_grad, axis=1, keepdims=True)
    )
    caption_direction = cap_inv * (
        cap_grad - cap_unit * jnp.sum(cap_unit * cap_grad, axis=1, keepdims=True)
    )
    query_ct = jnp.concatenate([figure_direction, caption_direction], axis=0)
    query_ct_rows, key_value_ct = pullback(query_ct)
    half = feature_width // 2
    onehot_three = jnp.concatenate([query_onehot] * 3, axis=0)
    grad_parts = []
    for part in range(2):
        cols = slice(part * half, (part + 1) * half)
        query_part = lax.dot_general(
            query_ct_rows,
            qkv_full[0][cols],
            (((1,), (1,)), ((), ())),
            preferred_element_type=jnp.float32,
        )
        slot_part = lax.dot_general(
            key_value_ct,
            kv_full[cols],
            (((1,), (1,)), ((), ())),
            preferred_element_type=jnp.float32,
        )
        scatter_src = query_part + query_ct[:, cols]
        piece_hi = lax.reduce_precision(scatter_src, exponent_bits=8, mantissa_bits=7)
        rest = scatter_src - piece_hi
        piece_mid = lax.reduce_precision(rest, exponent_bits=8, mantissa_bits=7)
        piece_lo = rest - piece_mid
        pieces = jnp.concatenate([piece_hi, piece_mid, piece_lo], axis=0).astype(jnp.bfloat16)
        scatter_part = lax.dot_general(
            onehot_three, pieces, (((0,), (0,)), ((), ())), preferred_element_type=jnp.float32
        )
        slot_gradient = (slot_part + scatter_part).astype(jnp.bfloat16)
        back_rows = jnp.einsum(
            "sop,sd->opd", recv_onehot, slot_gradient, preferred_element_type=jnp.float32
        ).astype(jnp.bfloat16)
        home_rows = lax.all_to_all(back_rows, "dp", split_axis=0, concat_axis=0, tiled=True)
        grad_parts.append(
            jnp.einsum(
                "opk,opd->kd", send_onehot, home_rows, preferred_element_type=jnp.float32
            ).astype(jnp.bfloat16)
        )
    page_grad = jnp.concatenate(grad_parts, axis=1)
    return (page_grad, pair_loss)


def solution(mesh):
    return jax.shard_map(
        body,
        mesh=mesh,
        in_specs=(
            P(("dp", "fsdp"), None),
            P(("dp", "fsdp")),
            P(("dp", "fsdp"), None),
            P(None, "fsdp", None),
            P(None, "fsdp"),
            P(("dp", "fsdp")),
            P(("dp", "fsdp")),
            P(),
            P(("dp", "fsdp")),
        ),
        out_specs=(P(("dp", "fsdp"), None), P(("dp", "fsdp"))),
        check_vma=False,
    )
```

profile of v0, /device:TPU:0, one launch (start us, length us, event | category | flops | bytes accessed | tf_op | source)
XLA Modules:
  0.0 259.1 jit_solution(14258695298128781325)
XLA Ops:
  8.7 1.4 reduce-window.6
  15.5 4.5 %add_convert_fusion = bf16[16,51,2048]{2,1,0:T(8,128)(2,1)} fusion(f32[16,1,2048]{2,1,0:T(1,128)S(1)} %scatter.15, bf16[640,2048]{1,0:T(8,128)(2,1)S(1)} %copy-done, pred[16,50,640]{2,1,0:T(8,128)(4,1)S(1)} %broadcast_compare_fusion), kind=kOutput, calls=%fused_computation.6 | convolution fusion | flops 2142437376 | bytes 6606848 | tf_op jit(solution)/shard_map/opk,kd->opd/dot_general | solution.py:87
  20.0 7.3 %all-to-all-start = ((bf16[16,51,2048]{2,1,0:T(8,128)(2,1)}), bf16[16,51,2048]{2,1,0:T(8,128)(2,1)}, u32[]{:S(2)}, u32[]{:S(2)}) async-start(bf16[16,51,2048]{2,1,0:T(8,128)(2,1)} %add_convert_fusion), calls=%async_computation | async-start | bytes 7340032 | tf_op jit(solution)/shard_map/all_to_all | solution.py:90
  28.9 1.7 scatter.19
  31.0 46.8 %all-to-all-done = bf16[16,51,2048]{2,1,0:T(8,128)(2,1)} async-done(((bf16[16,51,2048]{2,1,0:T(8,128)(2,1)}), bf16[16,51,2048]{2,1,0:T(8,128)(2,1)}, u32[]{:S(2)}, u32[]{:S(2)}) %all-to-all-start) | async-done | bytes 3342368 | tf_op jit(solution)/shard_map/all_to_all | solution.py:90
  79.0 5.1 %bitcast_convert_fusion = bf16[640,2048]{1,0:T(8,128)(2,1)S(1)} fusion(bf16[16,51,2048]{2,1,0:T(8,128)(2,1)} %all-to-all-done, s32[16,51]{1,0:T(8,128)S(1)} %concatenate.54), kind=kOutput, calls=%fused_computation.7 | convolution fusion | flops 2140928000 | bytes 5967040 | tf_op jit(solution)/shard_map/sop,opd->sd/dot_general | solution.py:99
  84.8 3.0 %fusion.37 = bf16[32,1024]{1,0:T(8,128)(2,1)S(1)} fusion(bf16[32,2048]{1,0:T(8,128)(2,1)S(1)} %convolution_convert_fusion, bf16[3,2048,1024]{2,1,0:T(8,128)(2,1)} %all-gather.3.cloned.1.call-done), kind=kOutput, calls=%fused_computation.71 | convolution fusion | flops 134250496 | bytes 4390912 | tf_op jit(solution)/shard_map/dot_general | solution.py:116
  87.9 4.2 %slice_bitcast_fusion.2 = (bf16[2048,1024]{1,0:T(8,128)(2,1)S(1)}, bf16[2048,1024]{1,0:T(8,128)(2,1)S(1)}) fusion(bf16[3,2048,1024]{2,1,0:T(8,128)(2,1)} %all-gather.3.cloned.1.call-done), kind=kLoop, calls=%fused_computation.14 | loop fusion | bytes 16777216 | tf_op jit(solution)/shard_map/squeeze | solution.py:106
  92.2 6.1 %fusion.8 = bf16[640,2048]{1,0:T(8,128)(2,1)S(1)} fusion(bf16[640,2048]{1,0:T(8,128)(2,1)S(1)} %bitcast_convert_fusion, bf16[2048,1024]{1,0:T(8,128)(2,1)S(1)} %get-tuple-element.57, bf16[2048,1024]{1,0:T(8,128)(2,1)S(1)} %get-tuple-element.58), kind=kOutput, calls=%fused_computation.16 | convolution fusion | flops 5386797056 | bytes 13631488 | tf_op jit(solution)/shard_map/dot_general | solution.py:119
  98.5 1.5 copy.42
  101.3 1.8 copy-done.7
  103.9 14.1 %all-gather.5.cloned.1.call-done = bf16[1024,2048]{1,0:T(8,128)(2,1)} async-done(((bf16[1024,256]{1,0:T(8,128)(2,1)}), bf16[1024,2048]{1,0:T(8,128)(2,1)}) %all-gather.5.cloned.1.call-update) | async-done | bytes 4194320 | tf_op jit(solution)/shard_map/all_gather | solution.py:104
  118.0 3.0 %convolution_add_fusion = f32[32,2048]{1,0:T(8,128)S(1)} fusion(bf16[32,1024]{1,0:T(8,128)(2,1)S(1)} %reshape.309, bf16[1024,2048]{1,0:T(8,128)(2,1)} %all-gather.5.cloned.1.call-done, bf16[32,2048]{1,0:T(8,128)(2,1)S(1)} %convolution_convert_fusion), kind=kOutput, calls=%fused_computation.27 | convolution fusion | flops 134348800 | bytes 4653056 | tf_op jit(solution)/shard_map/jvp()/dot_general | solution.py:31
  121.3 1.5 broadcast_in_dim.99
  122.8 6.8 %all-to-all-start.1 = ((bf16[16,32,2176]{2,1,0:T(8,128)(2,1)}), bf16[16,32,2176]{2,1,0:T(8,128)(2,1)S(1)}, u32[]{:S(2)}, u32[]{:S(2)}) async-start(bf16[16,32,2176]{2,1,0:T(8,128)(2,1)} %broadcast_in_dim.99), calls=%async_computation.1 | async-start | bytes 4456448 | tf_op jit(solution)/shard_map/all_to_all | solution.py:141
  131.6 30.2 %all-to-all-done.1 = bf16[16,32,2176]{2,1,0:T(8,128)(2,1)S(1)} async-done(((bf16[16,32,2176]{2,1,0:T(8,128)(2,1)}), bf16[16,32,2176]{2,1,0:T(8,128)(2,1)S(1)}, u32[]{:S(2)}, u32[]{:S(2)}) %all-to-all-start.1) | async-done | bytes 2228256 | tf_op jit(solution)/shard_map/all_to_all | solution.py:141
  167.3 1.7 fusion.26
  170.0 1.7 convolution_convert_fusion.1
  171.7 1.7 convolution_convert_fusion.2
  173.6 7.4 %fusion.5 = f32[640,1024]{1,0:T(8,128)} fusion(bf16[2048,1024]{1,0:T(8,128)(2,1)} %copy-done.9, bf16[2048,1024]{1,0:T(8,128)(2,1)} %copy-done.8, bf16[640,1024]{0,1:T(8,128)(2,1)} %bitcast.134, bf16[640,1024]{0,1:T(8,128)(2,1)} %bitcast.136), kind=kOutput, calls=%fused_computation.11 | convolution fusion | flops 2697986048 | bytes 13631488 | tf_op jit(solution)/shard_map/dot_general | solution.py:199
  181.1 2.3 reduce-precision_convert_fusion.1
  183.4 5.0 %fusion.16 = bf16[16,51,1024]{2,1,0:T(8,128)(2,1)} fusion(s32[16,51]{1,0:T(8,128)S(1)} %copy-done.18, f32[640,1024]{1,0:T(8,128)} %fusion.5, bf16[32,1024]{1,0:T(8,128)(2,1)S(1)} %get-tuple-element.71, bf16[32,1024]{1,0:T(8,128)(2,1)S(1)} %get-tuple-element.72, bf16[32,1024]{1,0:T(8,128)(2,1)S(1)} %get-tuple-element.70, pred[32,640]{1,0:T(32,128)(4,1)S(1)} %copy-done.16), kind=kOutput, calls=%fused_computation.39 | convolution fusion | flops 1198757888 | bytes 4512960 | tf_op jit(solution)/shard_map/sop,sd->opd/dot_general | solution.py:215
  188.5 5.1 %all-to-all-start.3 = ((bf16[16,51,1024]{2,1,0:T(8,128)(2,1)}), bf16[16,51,1024]{2,1,0:T(8,128)(2,1)S(1)}, u32[]{:S(2)}, u32[]{:S(2)}) async-start(bf16[16,51,1024]{2,1,0:T(8,128)(2,1)} %fusion.16), calls=%async_computation.3 | async-start | bytes 3670016 | tf_op jit(solution)/shard_map/all_to_all | solution.py:218
  193.6 2.5 reduce-precision_convert_fusion.3
  196.1 6.7 %fusion.2 = f32[640,1024]{1,0:T(8,128)} fusion(bf16[2048,1024]{1,0:T(8,128)(2,1)} %copy-done.9, bf16[2048,1024]{1,0:T(8,128)(2,1)} %copy-done.8, bf16[640,1024]{0,1:T(8,128)(2,1)S(1)} %bitcast.135, bf16[640,1024]{0,1:T(8,128)(2,1)S(1)} %bitcast.137), kind=kOutput, calls=%fused_computation.9 | convolution fusion | flops 2697986048 | bytes 13631488 | tf_op jit(solution)/shard_map/dot_general | solution.py:199
  202.8 5.0 %fusion.15 = bf16[16,51,1024]{2,1,0:T(8,128)(2,1)} fusion(s32[16,51]{1,0:T(8,128)S(1)} %copy-done.18, f32[640,1024]{1,0:T(8,128)} %fusion.2, bf16[32,1024]{1,0:T(8,128)(2,1)S(1)} %get-tuple-element.68, bf16[32,1024]{1,0:T(8,128)(2,1)S(1)} %get-tuple-element.69, bf16[32,1024]{1,0:T(8,128)(2,1)S(1)} %get-tuple-element.67, pred[32,640]{1,0:T(32,128)(4,1)S(1)} %copy-done.16), kind=kOutput, calls=%fused_computation.38 | convolution fusion | flops 1198757888 | bytes 4512960 | tf_op jit(solution)/shard_map/sop,sd->opd/dot_general | solution.py:215
  207.8 11.8 %all-to-all-done.3 = bf16[16,51,1024]{2,1,0:T(8,128)(2,1)S(1)} async-done(((bf16[16,51,1024]{2,1,0:T(8,128)(2,1)}), bf16[16,51,1024]{2,1,0:T(8,128)(2,1)S(1)}, u32[]{:S(2)}, u32[]{:S(2)}) %all-to-all-start.3) | async-done | bytes 1671200 | tf_op jit(solution)/shard_map/all_to_all | solution.py:218
  219.6 4.4 %all-to-all-start.2 = ((bf16[16,51,1024]{2,1,0:T(8,128)(2,1)}), bf16[16,51,1024]{2,1,0:T(8,128)(2,1)}, u32[]{:S(2)}, u32[]{:S(2)}) async-start(bf16[16,51,1024]{2,1,0:T(8,128)(2,1)} %fusion.15), calls=%async_computation.2 | async-start | bytes 3670016 | tf_op jit(solution)/shard_map/all_to_all | solution.py:218
  224.7 2.7 %bitcast_convert_fusion.1 = bf16[640,1024]{1,0:T(8,128)(2,1)} fusion(bf16[16,51,1024]{2,1,0:T(8,128)(2,1)S(1)} %all-to-all-done.3, pred[16,50,640]{2,1,0:T(8,128)(4,1)S(1)} %broadcast_compare_fusion), kind=kOutput, calls=%fused_computation.18 | convolution fusion | flops 1070202880 | bytes 3493888 | tf_op jit(solution)/shard_map/opk,opd->kd/dot_general | solution.py:220
  227.4 19.8 %all-to-all-done.2 = bf16[16,51,1024]{2,1,0:T(8,128)(2,1)} async-done(((bf16[16,51,1024]{2,1,0:T(8,128)(2,1)}), bf16[16,51,1024]{2,1,0:T(8,128)(2,1)}, u32[]{:S(2)}, u32[]{:S(2)}) %all-to-all-start.2) | async-done | bytes 1671200 | tf_op jit(solution)/shard_map/all_to_all | solution.py:218
  247.2 3.3 %bitcast_convert_fusion.2 = bf16[640,1024]{1,0:T(8,128)(2,1)S(1)} fusion(bf16[16,51,1024]{2,1,0:T(8,128)(2,1)} %all-to-all-done.2, pred[16,50,640]{2,1,0:T(8,128)(4,1)S(1)} %broadcast_compare_fusion), kind=kOutput, calls=%fused_computation.19 | convolution fusion | flops 1070202880 | bytes 3493888 | tf_op jit(solution)/shard_map/opk,opd->kd/dot_general | solution.py:220
  250.5 1.7 pad_maximum_fusion.4
  (125 shorter events, 21.8 us)
Async XLA Ops:
  7.2 8.4 %copy-start = (bf16[640,2048]{1,0:T(8,128)(2,1)S(1)}, bf16[640,2048]{1,0:T(8,128)(2,1)}, u32[]{:S(2)}) copy-start(bf16[640,2048]{1,0:T(8,128)(2,1)} %param.17) | copy-start | bytes 7864324
  7.2 77.6 %all-gather.3.cloned.1.call-start = ((), (), s32[]{:S(2)}) async-start(), calls=%async_computation.4 | async-start | bytes 14155776 | tf_op jit(solution)/shard_map/all_gather | solution.py:103
  20.0 8.1 %copy-start.22 = (f32[16]{0:T(128)S(1)}, f32[16]{0:T(128)}, u32[]{:S(2)}) copy-start(f32[16]{0:T(128)} %param.25) | copy-start | bytes 196
  20.0 8.2 %copy-start.19 = (s32[1,640]{1,0:T(1,128)S(1)}, s32[1,640]{1,0:T(1,128)}, u32[]{:S(2)}) copy-start(s32[1,640]{1,0:T(1,128)} %param.19) | copy-start | bytes 7684
  20.0 10.6 %copy-start.23 = (s32[16]{0:T(128)S(1)}, s32[16]{0:T(128)}, u32[]{:S(2)}) copy-start(s32[16]{0:T(128)} %param.23) | copy-start | bytes 196
  20.0 10.6 %copy-start.24 = (s32[16]{0:T(128)S(1)}, s32[16]{0:T(128)}, u32[]{:S(2)}) copy-start(s32[16]{0:T(128)} %param.22) | copy-start | bytes 196
  20.0 57.8 %all-to-all-start = ((bf16[16,51,2048]{2,1,0:T(8,128)(2,1)}), bf16[16,51,2048]{2,1,0:T(8,128)(2,1)}, u32[]{:S(2)}, u32[]{:S(2)}) async-start(bf16[16,51,2048]{2,1,0:T(8,128)(2,1)} %add_convert_fusion), calls=%async_computation | async-start | bytes 7340032 | tf_op jit(solution)/shard_map/all_to_all | solution.py:90
  27.3 90.7 %all-gather.5.cloned.1.call-start = ((), (), s32[]{:S(2)}) async-start(), calls=%async_computation.5 | async-start | bytes 4718592 | tf_op jit(solution)/shard_map/all_gather | solution.py:104
  30.6 48.4 %copy-start.14 = (bf16[32,128]{1,0:T(8,128)(2,1)}, bf16[32,128]{1,0:T(8,128)(2,1)S(1)}, u32[]{:S(2)}) copy-start(bf16[32,128]{1,0:T(8,128)(2,1)S(1)} %scatter.19) | copy-start | bytes 24580
  79.0 5.1 %copy-start.17 = (s32[16,51]{1,0:T(8,128)}, s32[16,51]{1,0:T(8,128)S(1)}, u32[]{:S(2)}) copy-start(s32[16,51]{1,0:T(8,128)S(1)} %concatenate.54) | copy-start | bytes 9796
  87.9 12.8 %copy-start.11 = (bf16[32,16,64]{2,1,0:T(8,128)(2,1)}, bf16[32,16,64]{2,1,0:T(8,128)(2,1)S(1)}, u32[]{:S(2)}) copy-start(bf16[32,16,64]{2,1,0:T(8,128)(2,1)S(1)} %reshape.307) | copy-start | bytes 196612
  92.1 6.1 %copy-start.8 = (bf16[2048,1024]{1,0:T(8,128)(2,1)}, bf16[2048,1024]{1,0:T(8,128)(2,1)S(1)}, u32[]{:S(2)}) copy-start(bf16[2048,1024]{1,0:T(8,128)(2,1)S(1)} %get-tuple-element.57) | copy-start | bytes 12582916
  92.1 6.1 %copy-start.9 = (bf16[2048,1024]{1,0:T(8,128)(2,1)}, bf16[2048,1024]{1,0:T(8,128)(2,1)S(1)}, u32[]{:S(2)}) copy-start(bf16[2048,1024]{1,0:T(8,128)(2,1)S(1)} %get-tuple-element.58) | copy-start | bytes 12582916
  100.7 2.9 %copy-start.5 = (bf16[640,1024]{0,1:T(8,128)(2,1)}, bf16[640,1024]{0,1:T(8,128)(2,1)S(1)}, u32[]{:S(2)}) copy-start(bf16[640,1024]{0,1:T(8,128)(2,1)S(1)} %copy.43) | copy-start | bytes 3932164
  100.7 2.3 copy-start.7
  101.3 2.4 copy-start.3
  103.9 17.4 %copy-start.15 = (bf16[32,128]{1,0:T(8,128)(2,1)S(1)}, bf16[32,128]{1,0:T(8,128)(2,1)}, u32[]{:S(2)}) copy-start(bf16[32,128]{1,0:T(8,128)(2,1)} %copy-done.14) | copy-start | bytes 24580
  122.8 39.0 %all-to-all-start.1 = ((bf16[16,32,2176]{2,1,0:T(8,128)(2,1)}), bf16[16,32,2176]{2,1,0:T(8,128)(2,1)S(1)}, u32[]{:S(2)}, u32[]{:S(2)}) async-start(bf16[16,32,2176]{2,1,0:T(8,128)(2,1)} %broadcast_in_dim.99), calls=%async_computation.1 | async-start | bytes 4456448 | tf_op jit(solution)/shard_map/all_to_all | solution.py:141
  130.3 33.0 %copy-start.20 = (s32[16]{0:T(128)}, s32[16]{0:T(128)S(1)}, u32[]{:S(2)}) copy-start(s32[16]{0:T(128)S(1)} %iota_add_fusion) | copy-start | bytes 196
  162.9 2.2 copy-start.2
  164.8 2.5 copy-start.4
  166.5 2.6 %copy-start.6 = (bf16[640,1024]{0,1:T(8,128)(2,1)S(1)}, bf16[640,1024]{0,1:T(8,128)(2,1)}, u32[]{:S(2)}) copy-start(bf16[640,1024]{0,1:T(8,128)(2,1)} %copy-done.5) | copy-start | bytes 3932164
  170.0 1.7 copy-start.13
  181.1 2.4 copy-start.16
  181.1 2.4 copy-start.18
  188.5 31.1 %all-to-all-start.3 = ((bf16[16,51,1024]{2,1,0:T(8,128)(2,1)}), bf16[16,51,1024]{2,1,0:T(8,128)(2,1)S(1)}, u32[]{:S(2)}, u32[]{:S(2)}) async-start(bf16[16,51,1024]{2,1,0:T(8,128)(2,1)} %fusion.16), calls=%async_computation.3 | async-start | bytes 3670016 | tf_op jit(solution)/shard_map/all_to_all | solution.py:218
  193.6 2.5 copy-start.25
  193.6 2.5 copy-start.26
  207.8 16.2 %copy-start.21 = (s32[16]{0:T(128)S(1)}, s32[16]{0:T(128)}, u32[]{:S(2)}) copy-start(s32[16]{0:T(128)} %copy-done.20) | copy-start | bytes 196
  219.6 27.6 %all-to-all-start.2 = ((bf16[16,51,1024]{2,1,0:T(8,128)(2,1)}), bf16[16,51,1024]{2,1,0:T(8,128)(2,1)}, u32[]{:S(2)}, u32[]{:S(2)}) async-start(bf16[16,51,1024]{2,1,0:T(8,128)(2,1)} %fusion.15), calls=%async_computation.2 | async-start | bytes 3670016 | tf_op jit(solution)/shard_map/all_to_all | solution.py:218
  247.2 3.3 %copy-start.10 = (bf16[640,1024]{1,0:T(8,128)(2,1)S(1)}, bf16[640,1024]{1,0:T(8,128)(2,1)}, u32[]{:S(2)}) copy-start(bf16[640,1024]{1,0:T(8,128)(2,1)} %bitcast_convert_fusion.1) | copy-start | bytes 3932164
  247.2 5.0 %copy-start.1 = (bf16[640,2048]{1,0:T(8,128)(2,1)S(1)}, bf16[640,2048]{1,0:T(8,128)(2,1)}, u32[]{:S(2)}) copy-start(bf16[640,2048]{1,0:T(8,128)(2,1)} %param.17) | copy-start | bytes 7864324
  (1 other events, 0.9 us)
Sparse Core Ops, SparseCore 0:
  9.7 69.9 all-gather.2
  81.4 36.5 all-gather.4
where the time goes:
time: 260 us; the launch traced here: 259 us
  waiting for transfers between devices  124 us (48%)
  matrix products  68.3 us (26%)
  starting transfers between devices  23.9 us (9%)
  local copies, waits for them, and re-layouts  15.7 us (6%)
  between operations  15.3 us (6%)
  other arithmetic  11.9 us (5%)
    all_to_all x1, waiting for transfers between devices, body(): lax.all_to_all(send_rows, 'dp', split_axis=0, concat_axis=0, tiled=True)  46.8 us
    all_to_all x2, waiting for transfers between devices, body(): lax.all_to_all(back_rows, 'dp', split_axis=0, concat_axis=0, tiled=True)  31.6 us
    all_to_all x1, waiting for transfers between devices, body(): lax.all_to_all(jnp.broadcast_to(both_emb[None], (dp_count,) + both_emb.sh...  30.2 us
    dot_general x2, matrix products, body(): lax.dot_general(key_value_ct, kv_full[cols], (((1,), (1,)), ((), ())), pr...  14.1 us
    all_gather x1, waiting for transfers between devices, body(): lax.all_gather(out_weight, 'fsdp', axis=1, tiled=True)  14.1 us
    dot_general x2, matrix products, body(): jnp.einsum('sop,sd->opd', recv_onehot, slot_gradient, preferred_element_t...  10 us
    all_to_all x2, starting transfers between devices, body(): lax.all_to_all(back_rows, 'dp', split_axis=0, concat_axis=0, tiled=True)  9.51 us
    all_to_all x1, starting transfers between devices, body(): lax.all_to_all(send_rows, 'dp', split_axis=0, concat_axis=0, tiled=True)  7.3 us
  transfers between devices with their start and end apart: 6, of which 5 were waited for; matrix products, arithmetic and copies ran while one was open for 22% of the time, Pallas kernels for 0%

commit v1 on v0

--- a/solution.py
+++ b/solution.py
@@ -54,6 +54,14 @@
     logit_scale,
     loss_cotangent,
 ):
+
+    def search_the_point(d0, shard_in, which_axis):
+        newest = tuple((shard_in for _ in range(lax.axis_size(which_axis))))
+        raw_out = jnp.stack(newest, 0)
+        all_values = lax.all_to_all(raw_out, which_axis, 0, 0)
+        front = jnp.concatenate(all_values, d0)
+        return front
+
     dp_count = lax.axis_size("dp")
     row_count = page_embed.shape[0]
     feature_width = page_embed.shape[1]
@@ -101,7 +109,7 @@
     ).astype(jnp.bfloat16)
     qkv_full, out_full = (
         lax.all_gather(qkv_weight, "fsdp", axis=1, tiled=True),
-        lax.all_gather(out_weight, "fsdp", axis=1, tiled=True),
+        search_the_point(1, out_weight, "fsdp"),
     )
     kv_full = jnp.concatenate([qkv_full[1], qkv_full[2]], axis=1)
     doc_row = doc_ids[0]

time: 260 us -> 281 us (1.081)
  starting transfers between devices: 23.9 us -> 32.7 us
  waiting for transfers between devices: 124 us -> 131 us
    all_to_all x0 -> x1, waiting for transfers between devices: none -> 24 us  [search_the_point(): all_values = lax.all_to_all(raw_out, which_axis, 0, 0)]
    all_gather x1 -> x0, waiting for transfers between devices: 14.1 us -> none  [body(): lax.all_gather(out_weight, 'fsdp', axis=1, tiled=True)]
    all_to_all x0 -> x1, starting transfers between devices: none -> 5.27 us  [search_the_point(): all_values = lax.all_to_all(raw_out, which_axis, 0, 0)]
    all_to_all x1, starting transfers between devices: 6.81 us -> 11.7 us  [body(): lax.all_to_all(jnp.broadcast_to(both_emb[None], (dp_count,) + both_emb.sh...]
where the time goes in v1:
time: 281 us; the launch traced here: 280 us
  waiting for transfers between devices  131 us (47%)
  matrix products  70.6 us (25%)
  starting transfers between devices  32.7 us (12%)
  local copies, waits for them, and re-layouts  17.9 us (6%)
  between operations  15.4 us (5%)
  other arithmetic  11.9 us (4%)
    all_to_all x1, waiting for transfers between devices, body(): lax.all_to_all(send_rows, 'dp', split_axis=0, concat_axis=0, tiled=True)  47.3 us
    all_to_all x1, waiting for transfers between devices, body(): lax.all_to_all(jnp.broadcast_to(both_emb[None], (dp_count,) + both_emb.sh...  29.7 us
    all_to_all x2, waiting for transfers between devices, body(): lax.all_to_all(back_rows, 'dp', split_axis=0, concat_axis=0, tiled=True)  29.6 us
    all_to_all x1, waiting for transfers between devices, search_the_point(): all_values = lax.all_to_all(raw_out, which_axis, 0, 0)  24 us
    dot_general x2, matrix products, body(): lax.dot_general(key_value_ct, kv_full[cols], (((1,), (1,)), ((), ())), pr...  14.1 us
    all_to_all x1, starting transfers between devices, body(): lax.all_to_all(jnp.broadcast_to(both_emb[None], (dp_count,) + both_emb.sh...  11.7 us
    dot_general x2, matrix products, body(): jnp.einsum('sop,sd->opd', recv_onehot, slot_gradient, preferred_element_t...  10 us
    all_to_all x2, starting transfers between devices, body(): lax.all_to_all(back_rows, 'dp', split_axis=0, concat_axis=0, tiled=True)  8.4 us
  transfers between devices with their start and end apart: 6, of which 5 were waited for; matrix products, arithmetic and copies ran while one was open for 22% of the time, Pallas kernels for 0%

profile of v1, /device:TPU:0, one launch (start us, length us, event | category | flops | bytes accessed | tf_op | source)
XLA Modules:
  0.0 279.7 jit_solution(1242019183952692527)
XLA Ops:
  15.5 4.5 %add_convert_fusion = bf16[16,51,2048]{2,1,0:T(8,128)(2,1)} fusion(f32[16,1,2048]{2,1,0:T(1,128)S(1)} %scatter.15, bf16[640,2048]{1,0:T(8,128)(2,1)S(1)} %copy-done, pred[16,50,640]{2,1,0:T(8,128)(4,1)S(1)} %broadcast_compare_fusion), kind=kOutput, calls=%fused_computation.6 | convolution fusion | flops 2142437376 | bytes 6606848 | tf_op jit(solution)/shard_map/opk,kd->opd/dot_general | solution.py:95
  20.0 7.3 %all-to-all-start = ((bf16[16,51,2048]{2,1,0:T(8,128)(2,1)}), bf16[16,51,2048]{2,1,0:T(8,128)(2,1)}, u32[]{:S(2)}, u32[]{:S(2)}) async-start(bf16[16,51,2048]{2,1,0:T(8,128)(2,1)} %add_convert_fusion), calls=%async_computation | async-start | bytes 7340032 | tf_op jit(solution)/shard_map/all_to_all | solution.py:98
  28.4 1.7 scatter.19
  30.5 47.3 %all-to-all-done = bf16[16,51,2048]{2,1,0:T(8,128)(2,1)} async-done(((bf16[16,51,2048]{2,1,0:T(8,128)(2,1)}), bf16[16,51,2048]{2,1,0:T(8,128)(2,1)}, u32[]{:S(2)}, u32[]{:S(2)}) %all-to-all-start) | async-done | bytes 3342368 | tf_op jit(solution)/shard_map/all_to_all | solution.py:98
  77.8 2.5 stack.2
  80.3 5.3 %all-to-all-start.1 = ((bf16[8,1024,256]{1,2,0:T(8,128)(2,1)}), bf16[8,1024,256]{1,2,0:T(8,128)(2,1)}, u32[]{:S(2)}, u32[]{:S(2)}) async-start(bf16[8,1024,256]{1,2,0:T(8,128)(2,1)} %stack.2), calls=%async_computation.1 | async-start | bytes 8388608 | tf_op jit(solution)/shard_map/all_to_all | solution.py:61
  86.8 5.1 %bitcast_convert_fusion = bf16[640,2048]{1,0:T(8,128)(2,1)S(1)} fusion(bf16[16,51,2048]{2,1,0:T(8,128)(2,1)} %all-to-all-done, s32[16,51]{1,0:T(8,128)S(1)} %concatenate.54), kind=kOutput, calls=%fused_computation.7 | convolution fusion | flops 2140928000 | bytes 5967040 | tf_op jit(solution)/shard_map/sop,opd->sd/dot_general | solution.py:107
  92.5 3.0 %fusion.37 = bf16[32,1024]{1,0:T(8,128)(2,1)S(1)} fusion(bf16[32,2048]{1,0:T(8,128)(2,1)S(1)} %convolution_convert_fusion, bf16[3,2048,1024]{2,1,0:T(8,128)(2,1)} %all-gather.2.cloned.1.call-done), kind=kOutput, calls=%fused_computation.71 | convolution fusion | flops 134250496 | bytes 4390912 | tf_op jit(solution)/shard_map/dot_general | solution.py:124
  95.7 4.0 %slice_bitcast_fusion.2 = (bf16[2048,1024]{1,0:T(8,128)(2,1)S(1)}, bf16[2048,1024]{1,0:T(8,128)(2,1)S(1)}) fusion(bf16[3,2048,1024]{2,1,0:T(8,128)(2,1)} %all-gather.2.cloned.1.call-done), kind=kLoop, calls=%fused_computation.14 | loop fusion | bytes 16777216 | tf_op jit(solution)/shard_map/squeeze | solution.py:114
  99.7 6.1 %fusion.8 = bf16[640,2048]{1,0:T(8,128)(2,1)S(1)} fusion(bf16[640,2048]{1,0:T(8,128)(2,1)S(1)} %bitcast_convert_fusion, bf16[2048,1024]{1,0:T(8,128)(2,1)S(1)} %get-tuple-element.57, bf16[2048,1024]{1,0:T(8,128)(2,1)S(1)} %get-tuple-element.58), kind=kOutput, calls=%fused_computation.16 | convolution fusion | flops 5386797056 | bytes 13631488 | tf_op jit(solution)/shard_map/dot_general | solution.py:127
  108.8 1.7 copy-done.6
  111.4 24.0 %all-to-all-done.1 = bf16[8,1024,256]{1,2,0:T(8,128)(2,1)} async-done(((bf16[8,1024,256]{1,2,0:T(8,128)(2,1)}), bf16[8,1024,256]{1,2,0:T(8,128)(2,1)}, u32[]{:S(2)}, u32[]{:S(2)}) %all-to-all-start.1) | async-done | bytes 4194336 | tf_op jit(solution)/shard_map/all_to_all | solution.py:61
  135.4 3.5 %convolution_add_fusion = f32[32,2048]{1,0:T(8,128)S(1)} fusion(bf16[32,1024]{1,0:T(8,128)(2,1)S(1)} %reshape.317, bf16[1024,2048]{0,1:T(8,128)(2,1)} %bitcast.11, bf16[32,2048]{1,0:T(8,128)(2,1)S(1)} %convolution_convert_fusion), kind=kOutput, calls=%fused_computation.27 | convolution fusion | flops 134348800 | bytes 4653056 | tf_op jit(solution)/shard_map/jvp()/dot_general | solution.py:31
  140.7 11.7 %all-to-all-start.2 = ((bf16[16,32,2176]{2,1,0:T(8,128)(2,1)}), bf16[16,32,2176]{2,1,0:T(8,128)(2,1)S(1)}, u32[]{:S(2)}, u32[]{:S(2)}) async-start(bf16[16,32,2176]{2,1,0:T(8,128)(2,1)} %broadcast_in_dim.99), calls=%async_computation.2 | async-start | bytes 4456448 | tf_op jit(solution)/shard_map/all_to_all | solution.py:149
  154.3 29.7 %all-to-all-done.2 = bf16[16,32,2176]{2,1,0:T(8,128)(2,1)S(1)} async-done(((bf16[16,32,2176]{2,1,0:T(8,128)(2,1)}), bf16[16,32,2176]{2,1,0:T(8,128)(2,1)S(1)}, u32[]{:S(2)}, u32[]{:S(2)}) %all-to-all-start.2) | async-done | bytes 2228256 | tf_op jit(solution)/shard_map/all_to_all | solution.py:149
  187.1 3.1 %convolution_convert_fusion.6 = bf16[32,1024]{1,0:T(8,128)(2,1)S(1)} fusion(bf16[1024,2048]{0,1:T(8,128)(2,1)} %bitcast.11, f32[16,2048]{1,0:T(8,128)S(1)} %get-tuple-element.64, f32[16,2048]{1,0:T(8,128)S(1)} %get-tuple-element.63), kind=kOutput, calls=%fused_computation.72 | convolution fusion | flops 134479872 | bytes 4521984 | tf_op jit(solution)/shard_map/transpose(jvp())/dot_general | solution.py:31
  191.0 1.7 fusion.26
  193.7 1.7 convolution_convert_fusion.1
  195.4 1.7 convolution_convert_fusion.2
  197.3 7.4 %fusion.5 = f32[640,1024]{1,0:T(8,128)} fusion(bf16[2048,1024]{1,0:T(8,128)(2,1)} %copy-done.8, bf16[2048,1024]{1,0:T(8,128)(2,1)} %copy-done.7, bf16[640,1024]{0,1:T(8,128)(2,1)} %bitcast.137, bf16[640,1024]{0,1:T(8,128)(2,1)} %bitcast.139), kind=kOutput, calls=%fused_computation.11 | convolution fusion | flops 2697986048 | bytes 13631488 | tf_op jit(solution)/shard_map/dot_general | solution.py:207
  204.8 2.3 reduce-precision_convert_fusion.1
  207.1 5.0 %fusion.16 = bf16[16,51,1024]{2,1,0:T(8,128)(2,1)} fusion(s32[16,51]{1,0:T(8,128)S(1)} %copy-done.18, f32[640,1024]{1,0:T(8,128)} %fusion.5, bf16[32,1024]{1,0:T(8,128)(2,1)S(1)} %get-tuple-element.71, bf16[32,1024]{1,0:T(8,128)(2,1)S(1)} %get-tuple-element.72, bf16[32,1024]{1,0:T(8,128)(2,1)S(1)} %get-tuple-element.70, pred[32,640]{1,0:T(32,128)(4,1)S(1)} %copy-done.16), kind=kOutput, calls=%fused_computation.39 | convolution fusion | flops 1198757888 | bytes 4512960 | tf_op jit(solution)/shard_map/sop,sd->opd/dot_general | solution.py:223
  212.2 4.0 %all-to-all-start.4 = ((bf16[16,51,1024]{2,1,0:T(8,128)(2,1)}), bf16[16,51,1024]{2,1,0:T(8,128)(2,1)S(1)}, u32[]{:S(2)}, u32[]{:S(2)}) async-start(bf16[16,51,1024]{2,1,0:T(8,128)(2,1)} %fusion.16), calls=%async_computation.4 | async-start | bytes 3670016 | tf_op jit(solution)/shard_map/all_to_all | solution.py:226
  216.2 2.5 reduce-precision_convert_fusion.3
  218.7 6.7 %fusion.2 = f32[640,1024]{1,0:T(8,128)} fusion(bf16[2048,1024]{1,0:T(8,128)(2,1)} %copy-done.8, bf16[2048,1024]{1,0:T(8,128)(2,1)} %copy-done.7, bf16[640,1024]{0,1:T(8,128)(2,1)S(1)} %bitcast.138, bf16[640,1024]{0,1:T(8,128)(2,1)S(1)} %bitcast.140), kind=kOutput, calls=%fused_computation.9 | convolution fusion | flops 2697986048 | bytes 13631488 | tf_op jit(solution)/shard_map/dot_general | solution.py:207
  225.4 5.0 %fusion.15 = bf16[16,51,1024]{2,1,0:T(8,128)(2,1)} fusion(s32[16,51]{1,0:T(8,128)S(1)} %copy-done.18, f32[640,1024]{1,0:T(8,128)} %fusion.2, bf16[32,1024]{1,0:T(8,128)(2,1)S(1)} %get-tuple-element.68, bf16[32,1024]{1,0:T(8,128)(2,1)S(1)} %get-tuple-element.69, bf16[32,1024]{1,0:T(8,128)(2,1)S(1)} %get-tuple-element.67, pred[32,640]{1,0:T(32,128)(4,1)S(1)} %copy-done.16), kind=kOutput, calls=%fused_computation.38 | convolution fusion | flops 1198757888 | bytes 4512960 | tf_op jit(solution)/shard_map/sop,sd->opd/dot_general | solution.py:223
  230.4 9.7 %all-to-all-done.4 = bf16[16,51,1024]{2,1,0:T(8,128)(2,1)S(1)} async-done(((bf16[16,51,1024]{2,1,0:T(8,128)(2,1)}), bf16[16,51,1024]{2,1,0:T(8,128)(2,1)S(1)}, u32[]{:S(2)}, u32[]{:S(2)}) %all-to-all-start.4) | async-done | bytes 1671200 | tf_op jit(solution)/shard_map/all_to_all | solution.py:226
  240.1 4.4 %all-to-all-start.3 = ((bf16[16,51,1024]{2,1,0:T(8,128)(2,1)}), bf16[16,51,1024]{2,1,0:T(8,128)(2,1)}, u32[]{:S(2)}, u32[]{:S(2)}) async-start(bf16[16,51,1024]{2,1,0:T(8,128)(2,1)} %fusion.15), calls=%async_computation.3 | async-start | bytes 3670016 | tf_op jit(solution)/shard_map/all_to_all | solution.py:226
  245.3 2.7 bitcast_convert_fusion.1
  247.9 19.9 %all-to-all-done.3 = bf16[16,51,1024]{2,1,0:T(8,128)(2,1)} async-done(((bf16[16,51,1024]{2,1,0:T(8,128)(2,1)}), bf16[16,51,1024]{2,1,0:T(8,128)(2,1)}, u32[]{:S(2)}, u32[]{:S(2)}) %all-to-all-start.3) | async-done | bytes 1671200 | tf_op jit(solution)/shard_map/all_to_all | solution.py:226
  267.8 3.3 %bitcast_convert_fusion.2 = bf16[640,1024]{1,0:T(8,128)(2,1)S(1)} fusion(bf16[16,51,1024]{2,1,0:T(8,128)(2,1)} %all-to-all-done.3, pred[16,50,640]{2,1,0:T(8,128)(4,1)S(1)} %broadcast_compare_fusion), kind=kOutput, calls=%fused_computation.19 | convolution fusion | flops 1070202880 | bytes 3493888 | tf_op jit(solution)/shard_map/opk,opd->kd/dot_general | solution.py:228
  271.1 1.7 pad_maximum_fusion.4
  (126 shorter events, 24.1 us)
Async XLA Ops:
  7.2 8.4 %copy-start = (bf16[640,2048]{1,0:T(8,128)(2,1)S(1)}, bf16[640,2048]{1,0:T(8,128)(2,1)}, u32[]{:S(2)}) copy-start(bf16[640,2048]{1,0:T(8,128)(2,1)} %param.17) | copy-start | bytes 7864324
  7.2 85.4 %all-gather.2.cloned.1.call-start = ((), (), s32[]{:S(2)}) async-start(), calls=%async_computation.5 | async-start | bytes 14155776 | tf_op jit(solution)/shard_map/all_gather | solution.py:111
  20.0 7.3 %copy-start.22 = (f32[16]{0:T(128)S(1)}, f32[16]{0:T(128)}, u32[]{:S(2)}) copy-start(f32[16]{0:T(128)} %param.25) | copy-start | bytes 196
  20.0 7.5 %copy-start.19 = (s32[1,640]{1,0:T(1,128)S(1)}, s32[1,640]{1,0:T(1,128)}, u32[]{:S(2)}) copy-start(s32[1,640]{1,0:T(1,128)} %param.19) | copy-start | bytes 7684
  20.0 7.6 %copy-start.12 = (bf16[1024,256]{1,0:T(8,128)(2,1)S(1)}, bf16[1024,256]{1,0:T(8,128)(2,1)}, u32[]{:S(2)}) copy-start(bf16[1024,256]{1,0:T(8,128)(2,1)} %param.21) | copy-start | bytes 1572868
  20.0 10.1 %copy-start.23 = (s32[16]{0:T(128)S(1)}, s32[16]{0:T(128)}, u32[]{:S(2)}) copy-start(s32[16]{0:T(128)} %param.23) | copy-start | bytes 196
  20.0 10.1 %copy-start.24 = (s32[16]{0:T(128)S(1)}, s32[16]{0:T(128)}, u32[]{:S(2)}) copy-start(s32[16]{0:T(128)} %param.22) | copy-start | bytes 196
  20.0 57.8 %all-to-all-start = ((bf16[16,51,2048]{2,1,0:T(8,128)(2,1)}), bf16[16,51,2048]{2,1,0:T(8,128)(2,1)}, u32[]{:S(2)}, u32[]{:S(2)}) async-start(bf16[16,51,2048]{2,1,0:T(8,128)(2,1)} %add_convert_fusion), calls=%async_computation | async-start | bytes 7340032 | tf_op jit(solution)/shard_map/all_to_all | solution.py:98
  30.1 50.2 %copy-start.14 = (bf16[32,128]{1,0:T(8,128)(2,1)}, bf16[32,128]{1,0:T(8,128)(2,1)S(1)}, u32[]{:S(2)}) copy-start(bf16[32,128]{1,0:T(8,128)(2,1)S(1)} %scatter.19) | copy-start | bytes 24580
  80.3 55.0 %all-to-all-start.1 = ((bf16[8,1024,256]{1,2,0:T(8,128)(2,1)}), bf16[8,1024,256]{1,2,0:T(8,128)(2,1)}, u32[]{:S(2)}, u32[]{:S(2)}) async-start(bf16[8,1024,256]{1,2,0:T(8,128)(2,1)} %stack.2), calls=%async_computation.1 | async-start | bytes 8388608 | tf_op jit(solution)/shard_map/all_to_all | solution.py:61
  86.8 5.1 %copy-start.17 = (s32[16,51]{1,0:T(8,128)}, s32[16,51]{1,0:T(8,128)S(1)}, u32[]{:S(2)}) copy-start(s32[16,51]{1,0:T(8,128)S(1)} %concatenate.54) | copy-start | bytes 9796
  95.7 12.6 %copy-start.10 = (bf16[32,16,64]{2,1,0:T(8,128)(2,1)}, bf16[32,16,64]{2,1,0:T(8,128)(2,1)S(1)}, u32[]{:S(2)}) copy-start(bf16[32,16,64]{2,1,0:T(8,128)(2,1)S(1)} %reshape.315) | copy-start | bytes 196612
  99.7 6.1 %copy-start.7 = (bf16[2048,1024]{1,0:T(8,128)(2,1)}, bf16[2048,1024]{1,0:T(8,128)(2,1)S(1)}, u32[]{:S(2)}) copy-start(bf16[2048,1024]{1,0:T(8,128)(2,1)S(1)} %get-tuple-element.57) | copy-start | bytes 12582916
  99.7 6.1 %copy-start.8 = (bf16[2048,1024]{1,0:T(8,128)(2,1)}, bf16[2048,1024]{1,0:T(8,128)(2,1)S(1)}, u32[]{:S(2)}) copy-start(bf16[2048,1024]{1,0:T(8,128)(2,1)S(1)} %get-tuple-element.58) | copy-start | bytes 12582916
  108.3 2.9 %copy-start.4 = (bf16[640,1024]{0,1:T(8,128)(2,1)}, bf16[640,1024]{0,1:T(8,128)(2,1)S(1)}, u32[]{:S(2)}) copy-start(bf16[640,1024]{0,1:T(8,128)(2,1)S(1)} %copy.45) | copy-start | bytes 3932164
  108.3 2.3 copy-start.6
  108.8 2.4 copy-start.2
  135.4 3.8 %copy-start.15 = (bf16[32,128]{1,0:T(8,128)(2,1)S(1)}, bf16[32,128]{1,0:T(8,128)(2,1)}, u32[]{:S(2)}) copy-start(bf16[32,128]{1,0:T(8,128)(2,1)} %copy-done.14) | copy-start | bytes 24580
  140.7 43.3 %all-to-all-start.2 = ((bf16[16,32,2176]{2,1,0:T(8,128)(2,1)}), bf16[16,32,2176]{2,1,0:T(8,128)(2,1)S(1)}, u32[]{:S(2)}, u32[]{:S(2)}) async-start(bf16[16,32,2176]{2,1,0:T(8,128)(2,1)} %broadcast_in_dim.99), calls=%async_computation.2 | async-start | bytes 4456448 | tf_op jit(solution)/shard_map/all_to_all | solution.py:149
  153.1 32.5 %copy-start.20 = (s32[16]{0:T(128)}, s32[16]{0:T(128)S(1)}, u32[]{:S(2)}) copy-start(s32[16]{0:T(128)S(1)} %iota_add_fusion) | copy-start | bytes 196
  187.0 4.0 %copy-start.3 = (f32[16,32,640]{2,1,0:T(8,128)S(1)}, f32[16,32,640]{2,1,0:T(8,128)}, u32[]{:S(2)}) copy-start(f32[16,32,640]{2,1,0:T(8,128)} %copy-done.2) | copy-start | bytes 3932164
  190.2 2.6 copy-start.5
  193.7 1.7 copy-start.13
  204.8 2.4 copy-start.16
  204.8 2.4 copy-start.18
  212.2 28.0 %all-to-all-start.4 = ((bf16[16,51,1024]{2,1,0:T(8,128)(2,1)}), bf16[16,51,1024]{2,1,0:T(8,128)(2,1)S(1)}, u32[]{:S(2)}, u32[]{:S(2)}) async-start(bf16[16,51,1024]{2,1,0:T(8,128)(2,1)} %fusion.16), calls=%async_computation.4 | async-start | bytes 3670016 | tf_op jit(solution)/shard_map/all_to_all | solution.py:226
  216.2 2.5 copy-start.25
  216.2 2.5 copy-start.26
  230.4 14.2 %copy-start.21 = (s32[16]{0:T(128)S(1)}, s32[16]{0:T(128)}, u32[]{:S(2)}) copy-start(s32[16]{0:T(128)} %copy-done.20) | copy-start | bytes 196
  240.1 27.7 %all-to-all-start.3 = ((bf16[16,51,1024]{2,1,0:T(8,128)(2,1)}), bf16[16,51,1024]{2,1,0:T(8,128)(2,1)}, u32[]{:S(2)}, u32[]{:S(2)}) async-start(bf16[16,51,1024]{2,1,0:T(8,128)(2,1)} %fusion.15), calls=%async_computation.3 | async-start | bytes 3670016 | tf_op jit(solution)/shard_map/all_to_all | solution.py:226
  267.8 3.3 %copy-start.9 = (bf16[640,1024]{1,0:T(8,128)(2,1)S(1)}, bf16[640,1024]{1,0:T(8,128)(2,1)}, u32[]{:S(2)}) copy-start(bf16[640,1024]{1,0:T(8,128)(2,1)} %bitcast_convert_fusion.1) | copy-start | bytes 3932164
  267.8 5.0 %copy-start.1 = (bf16[640,2048]{1,0:T(8,128)(2,1)S(1)}, bf16[640,2048]{1,0:T(8,128)(2,1)}, u32[]{:S(2)}) copy-start(bf16[640,2048]{1,0:T(8,128)(2,1)} %param.17) | copy-start | bytes 7864324
  (1 other events, 0.9 us)
Sparse Core Ops, SparseCore 0:
  9.7 69.9 all-gather.1
